TPU v7x, 512 devices: a whole 4x4x16 slice. The times are simulated.
512 devices in a mesh: pipe: 16 (over z), seq: 8 (over y, core), dp: 4 (over x).
Axes of the slice: x: 4, y: 4, z: 16, core: 2. Of those that a mesh axis runs over, the one named last changes fastest.
Arguments:
- acts: bfloat16 [16, 4, 1024, 8192], P('pipe', 'dp', 'seq'), may hold values from -6 to 6
- top_grad: bfloat16 [4, 1024, 8192], P('dp', 'seq'), may hold values from -6 to 6
- a_rows: bfloat16 [16, 32, 8192], P('pipe', None, ('seq', 'dp')), may hold values from -1 to 1
- b_rows: bfloat16 [16, 32, 8192], P('pipe', None, ('seq', 'dp')), may hold values from -0.375 to 0.375
- gain: bfloat16 [16, 8192], P('pipe', ('seq', 'dp')), may hold values from 0.5 to 1.5
Outputs:
- grad_a: float32 [16, 32, 8192], P('pipe', None, ('seq', 'dp'))
- grad_b: float32 [16, 32, 8192], P('pipe', None, ('seq', 'dp'))
- grad_gain: float32 [16, 8192], P('pipe', ('seq', 'dp'))
- clip_factors: float32 [4], P('dp')
All inputs are finite; a program needn't handle non-finite values.
Results may differ from a plain program's by a relative error of at most 0.019.
Values may be sent and summed in bfloat16 or wider, within the bound.
No kernel may reach another device: no remote copies, remote signals or barrier semaphores. Data moves between devices by JAX's collectives and lax.ppermute only.
A program may use at most 64 MiB of HBM per device.

v0:
```python
import math
import jax
import jax.numpy as jnp
from jax import lax
from jax.sharding import PartitionSpec as P

rows_per_block = 16


def from_behind(value, axis, steps):
    count = lax.axis_size(axis)
    initial, last = (max(0, -steps), min(count, count - steps))
    return lax.ppermute(value, axis, [(source, source + steps) for source in range(initial, last)])


def on_device(acts, top_grad, a_rows, b_rows, gain):
    sections = lax.axis_size("pipe")
    section = lax.axis_index("pipe")
    hidden = acts[0, 0]
    top = top_grad[0]
    rank = a_rows.shape[1]
    params = jnp.concatenate([a_rows[0], b_rows[0], gain], axis=0)
    whole = lax.all_gather(params, ("seq", "dp"), axis=1, tiled=True)
    a_full = whole[:rank]
    b_full = whole[rank : 2 * rank]
    gain_float = whole[2 * rank].astype(jnp.float32)
    rows, width = hidden.shape
    block_total = rows // rows_per_block
    hidden_float = hidden.astype(jnp.float32)
    inverse_root_mean = jnp.sqrt(
        jnp.mean(hidden_float * hidden_float, axis=-1, keepdims=True) + 1e-05
    )
    input_normalized = hidden_float / inverse_root_mean
    normalized_rows = (input_normalized * gain_float).astype(jnp.bfloat16)
    low = jnp.dot(normalized_rows, a_full.T, preferred_element_type=jnp.float32).astype(
        jnp.bfloat16
    )
    contract_last = (((1,), (1,)), ((), ()))
    contract_first = (((0,), (0,)), ((), ()))

    def back_block(upstream_gradient, block_offset):
        hidden_part = lax.dynamic_slice_in_dim(hidden, block_offset, rows_per_block, 0)
        r_part = lax.dynamic_slice_in_dim(inverse_root_mean, block_offset, rows_per_block, 0)
        input_portion = hidden_part.astype(jnp.float32) / r_part
        d_low = lax.dot_general(
            upstream_gradient, b_full, contract_last, preferred_element_type=jnp.float32
        ).astype(jnp.bfloat16)
        normalized_gradient = jnp.dot(d_low, a_full, preferred_element_type=jnp.float32)
        input_gradient = normalized_gradient * gain_float
        hidden_gradient = (
            upstream_gradient.astype(jnp.float32)
            + (
                input_gradient
                - input_portion * jnp.mean(input_gradient * input_portion, axis=-1, keepdims=True)
            )
            / r_part
        )
        return hidden_gradient.astype(jnp.bfloat16)

    def turn(turn_index, carry):
        incoming, store = carry
        block_index = turn_index - (sections - 1 - section)
        inside = jnp.logical_and(block_index >= 0, block_index < block_total)
        block_offset = jnp.clip(block_index, 0, block_total - 1) * rows_per_block
        top_block = lax.dynamic_slice_in_dim(top, block_offset, rows_per_block, 0)
        source = jnp.where(section == sections - 1, top_block, incoming)
        slot = jnp.where(inside, block_index, block_total)
        store = lax.dynamic_update_slice_in_dim(store, source[None], slot, 0)
        result = back_block(source, block_offset)
        incoming = from_behind(result, "pipe", -1)
        return (incoming, store)

    begin = (
        jnp.zeros((rows_per_block, width), jnp.bfloat16),
        jnp.zeros((block_total + 1, rows_per_block, width), jnp.bfloat16),
    )
    store = lax.fori_loop(0, sections + block_total - 1, turn, begin)[1]
    mine = store[:block_total].reshape(rows, width)
    d_low = lax.dot_general(mine, b_full, contract_last, preferred_element_type=jnp.float32).astype(
        jnp.bfloat16
    )
    normalized_gradient = jnp.dot(d_low, a_full, preferred_element_type=jnp.float32)
    grad_a = lax.dot_general(
        d_low, normalized_rows, contract_first, preferred_element_type=jnp.float32
    )
    grad_b = lax.dot_general(low, mine, contract_first, preferred_element_type=jnp.float32)
    gain_gradient = jnp.sum(normalized_gradient * input_normalized, axis=0)[None, :]
    grads = jnp.concatenate([grad_a, grad_b, gain_gradient], axis=0)
    part = lax.psum_scatter(grads, "seq", scatter_dimension=1, tiled=True)
    examples = lax.axis_size("dp")
    example = lax.axis_index("dp")
    square = jnp.sum(part * part)
    squares = jnp.where(jnp.arange(examples) == example, square, 0.0).astype(jnp.float32)
    totals = lax.psum(squares, ("pipe", "seq", "dp"))
    bound = math.sqrt(sections * (2 * rank + 1) * width)
    factors = bound / (jnp.sqrt(totals) + 0.01 * bound)
    gathered = lax.all_gather(part, "dp", axis=0, tiled=False)
    share = part.shape[1] // examples
    pieces = lax.dynamic_slice_in_dim(gathered, example * share, share, 2)
    combined = jnp.sum(factors[:, None, None] * pieces, axis=0)
    out_a = combined[:rank]
    out_b = combined[rank : 2 * rank]
    out_g = combined[2 * rank :]
    factor = lax.dynamic_slice_in_dim(factors, example, 1, 0)
    return (out_a[None], out_b[None], out_g, factor)


def solution(mesh):
    in_specs = (
        P("pipe", "dp", "seq", None),
        P("dp", "seq", None),
        P("pipe", None, ("seq", "dp")),
        P("pipe", None, ("seq", "dp")),
        P("pipe", ("seq", "dp")),
    )
    out_specs = (
        P("pipe", None, ("seq", "dp")),
        P("pipe", None, ("seq", "dp")),
        P("pipe", ("seq", "dp")),
        P("dp"),
    )
    return jax.shard_map(
        on_device, mesh=mesh, in_specs=in_specs, out_specs=out_specs, check_vma=False
    )
```

profile of v0, /device:TPU:1, one launch (start us, length us, event | category | flops | bytes accessed | tf_op | source)
XLA Modules:
  0.0 594.1 jit_solution(15978239011922078406)
XLA Ops:
  8.7 2.1 fusion.1
  10.8 64.3 %all-gather.5.cloned.1.call-done = bf16[65,8192]{1,0:T(8,128)(2,1)} async-done(((bf16[65,256]{1,0:T(8,128)(2,1)}), bf16[65,8192]{1,0:T(8,128)(2,1)}) %all-gather.5.cloned.1.call-update) | async-done | bytes 1064976 | tf_op jit(solution)/shard_map/all_gather | solution.py:23
  76.0 2.2 fusion.11
  78.5 318.4 %while.17 = (s32[]{:T(128)}, bf16[16,8192]{1,0:T(8,128)(2,1)S(1)}, bf16[9,16,8192]{2,1,0:T(8,128)(2,1)S(1)}, pred[]{:T(512)}, s32[]{:T(128)}, /*index=5*/bf16[12...) while((s32[]{:T(128)}, bf16[16,8192]{1,0:T(8,128)(2,1)S(1)}, ...), condition=%wide.region_3.4_spmd, body=%wide.region_1.3_spmd.sunk | while | flops 18612752 | bytes 5538680 | solution.py:77
  79.6 2.0 multiply_reduce_fusion.3
  84.7 8.4 %collective-permute-done = bf16[16,8192]{1,0:T(8,128)(2,1)S(1)} collective-permute-done((bf16[16,8192]{1,0:T(8,128)(2,1)}, bf16[16,8192]{1,0:T(8,128)(2,1)S(1)}, u32[]{:S(2)}, u32[]{:S(2)}) %collective-permute-start) | collective-permute-done | bytes 262176 | tf_op jit(solution)/shard_map/while/body/eval_jaxpr/ppermute | solution.py:13
  94.2 2.0 multiply_reduce_fusion.3
  99.3 7.5 %collective-permute-done = bf16[16,8192]{1,0:T(8,128)(2,1)S(1)} collective-permute-done((bf16[16,8192]{1,0:T(8,128)(2,1)}, bf16[16,8192]{1,0:T(8,128)(2,1)S(1)}, u32[]{:S(2)}, u32[]{:S(2)}) %collective-permute-start) | collective-permute-done | bytes 262176 | tf_op jit(solution)/shard_map/while/body/eval_jaxpr/ppermute | solution.py:13
  107.9 2.0 multiply_reduce_fusion.3
  113.0 6.7 %collective-permute-done = bf16[16,8192]{1,0:T(8,128)(2,1)S(1)} collective-permute-done((bf16[16,8192]{1,0:T(8,128)(2,1)}, bf16[16,8192]{1,0:T(8,128)(2,1)S(1)}, u32[]{:S(2)}, u32[]{:S(2)}) %collective-permute-start) | collective-permute-done | bytes 262176 | tf_op jit(solution)/shard_map/while/body/eval_jaxpr/ppermute | solution.py:13
  120.8 2.0 multiply_reduce_fusion.3
  125.9 8.2 %collective-permute-done = bf16[16,8192]{1,0:T(8,128)(2,1)S(1)} collective-permute-done((bf16[16,8192]{1,0:T(8,128)(2,1)}, bf16[16,8192]{1,0:T(8,128)(2,1)S(1)}, u32[]{:S(2)}, u32[]{:S(2)}) %collective-permute-start) | collective-permute-done | bytes 262176 | tf_op jit(solution)/shard_map/while/body/eval_jaxpr/ppermute | solution.py:13
  140.3 6.4 %collective-permute-done = bf16[16,8192]{1,0:T(8,128)(2,1)S(1)} collective-permute-done((bf16[16,8192]{1,0:T(8,128)(2,1)}, bf16[16,8192]{1,0:T(8,128)(2,1)S(1)}, u32[]{:S(2)}, u32[]{:S(2)}) %collective-permute-start) | collective-permute-done | bytes 262176 | tf_op jit(solution)/shard_map/while/body/eval_jaxpr/ppermute | solution.py:13
  147.8 2.0 multiply_reduce_fusion.3
  152.9 6.6 %collective-permute-done = bf16[16,8192]{1,0:T(8,128)(2,1)S(1)} collective-permute-done((bf16[16,8192]{1,0:T(8,128)(2,1)}, bf16[16,8192]{1,0:T(8,128)(2,1)S(1)}, u32[]{:S(2)}, u32[]{:S(2)}) %collective-permute-start) | collective-permute-done | bytes 262176 | tf_op jit(solution)/shard_map/while/body/eval_jaxpr/ppermute | solution.py:13
  165.7 7.2 %collective-permute-done = bf16[16,8192]{1,0:T(8,128)(2,1)S(1)} collective-permute-done((bf16[16,8192]{1,0:T(8,128)(2,1)}, bf16[16,8192]{1,0:T(8,128)(2,1)S(1)}, u32[]{:S(2)}, u32[]{:S(2)}) %collective-permute-start) | collective-permute-done | bytes 262176 | tf_op jit(solution)/shard_map/while/body/eval_jaxpr/ppermute | solution.py:13
  174.0 2.0 multiply_reduce_fusion.3
  179.1 7.2 %collective-permute-done = bf16[16,8192]{1,0:T(8,128)(2,1)S(1)} collective-permute-done((bf16[16,8192]{1,0:T(8,128)(2,1)}, bf16[16,8192]{1,0:T(8,128)(2,1)S(1)}, u32[]{:S(2)}, u32[]{:S(2)}) %collective-permute-start) | collective-permute-done | bytes 262176 | tf_op jit(solution)/shard_map/while/body/eval_jaxpr/ppermute | solution.py:13
  192.5 7.2 %collective-permute-done = bf16[16,8192]{1,0:T(8,128)(2,1)S(1)} collective-permute-done((bf16[16,8192]{1,0:T(8,128)(2,1)}, bf16[16,8192]{1,0:T(8,128)(2,1)S(1)}, u32[]{:S(2)}, u32[]{:S(2)}) %collective-permute-start) | collective-permute-done | bytes 262176 | tf_op jit(solution)/shard_map/while/body/eval_jaxpr/ppermute | solution.py:13
  200.9 2.0 multiply_reduce_fusion.3
  206.0 7.2 %collective-permute-done = bf16[16,8192]{1,0:T(8,128)(2,1)S(1)} collective-permute-done((bf16[16,8192]{1,0:T(8,128)(2,1)}, bf16[16,8192]{1,0:T(8,128)(2,1)S(1)}, u32[]{:S(2)}, u32[]{:S(2)}) %collective-permute-start) | collective-permute-done | bytes 262176 | tf_op jit(solution)/shard_map/while/body/eval_jaxpr/ppermute | solution.py:13
  219.4 7.2 %collective-permute-done = bf16[16,8192]{1,0:T(8,128)(2,1)S(1)} collective-permute-done((bf16[16,8192]{1,0:T(8,128)(2,1)}, bf16[16,8192]{1,0:T(8,128)(2,1)S(1)}, u32[]{:S(2)}, u32[]{:S(2)}) %collective-permute-start) | collective-permute-done | bytes 262176 | tf_op jit(solution)/shard_map/while/body/eval_jaxpr/ppermute | solution.py:13
  227.7 2.0 multiply_reduce_fusion.3
  232.8 7.2 %collective-permute-done = bf16[16,8192]{1,0:T(8,128)(2,1)S(1)} collective-permute-done((bf16[16,8192]{1,0:T(8,128)(2,1)}, bf16[16,8192]{1,0:T(8,128)(2,1)S(1)}, u32[]{:S(2)}, u32[]{:S(2)}) %collective-permute-start) | collective-permute-done | bytes 262176 | tf_op jit(solution)/shard_map/while/body/eval_jaxpr/ppermute | solution.py:13
  246.3 8.4 %collective-permute-done = bf16[16,8192]{1,0:T(8,128)(2,1)S(1)} collective-permute-done((bf16[16,8192]{1,0:T(8,128)(2,1)}, bf16[16,8192]{1,0:T(8,128)(2,1)S(1)}, u32[]{:S(2)}, u32[]{:S(2)}) %collective-permute-start) | collective-permute-done | bytes 262176 | tf_op jit(solution)/shard_map/while/body/eval_jaxpr/ppermute | solution.py:13
  255.8 2.0 multiply_reduce_fusion.3
  260.9 10.0 %collective-permute-done = bf16[16,8192]{1,0:T(8,128)(2,1)S(1)} collective-permute-done((bf16[16,8192]{1,0:T(8,128)(2,1)}, bf16[16,8192]{1,0:T(8,128)(2,1)S(1)}, u32[]{:S(2)}, u32[]{:S(2)}) %collective-permute-start) | collective-permute-done | bytes 262176 | tf_op jit(solution)/shard_map/while/body/eval_jaxpr/ppermute | solution.py:13
  272.0 2.0 multiply_reduce_fusion.3
  277.1 10.7 %collective-permute-done = bf16[16,8192]{1,0:T(8,128)(2,1)S(1)} collective-permute-done((bf16[16,8192]{1,0:T(8,128)(2,1)}, bf16[16,8192]{1,0:T(8,128)(2,1)S(1)}, u32[]{:S(2)}, u32[]{:S(2)}) %collective-permute-start) | collective-permute-done | bytes 262176 | tf_op jit(solution)/shard_map/while/body/eval_jaxpr/ppermute | solution.py:13
  288.8 2.0 multiply_reduce_fusion.3
  294.0 9.9 %collective-permute-done = bf16[16,8192]{1,0:T(8,128)(2,1)S(1)} collective-permute-done((bf16[16,8192]{1,0:T(8,128)(2,1)}, bf16[16,8192]{1,0:T(8,128)(2,1)S(1)}, u32[]{:S(2)}, u32[]{:S(2)}) %collective-permute-start) | collective-permute-done | bytes 262176 | tf_op jit(solution)/shard_map/while/body/eval_jaxpr/ppermute | solution.py:13
  305.0 2.0 multiply_reduce_fusion.3
  310.1 7.9 %collective-permute-done = bf16[16,8192]{1,0:T(8,128)(2,1)S(1)} collective-permute-done((bf16[16,8192]{1,0:T(8,128)(2,1)}, bf16[16,8192]{1,0:T(8,128)(2,1)S(1)}, u32[]{:S(2)}, u32[]{:S(2)}) %collective-permute-start) | collective-permute-done | bytes 262176 | tf_op jit(solution)/shard_map/while/body/eval_jaxpr/ppermute | solution.py:13
  319.1 2.0 multiply_reduce_fusion.3
  324.2 6.7 %collective-permute-done = bf16[16,8192]{1,0:T(8,128)(2,1)S(1)} collective-permute-done((bf16[16,8192]{1,0:T(8,128)(2,1)}, bf16[16,8192]{1,0:T(8,128)(2,1)S(1)}, u32[]{:S(2)}, u32[]{:S(2)}) %collective-permute-start) | collective-permute-done | bytes 262176 | tf_op jit(solution)/shard_map/while/body/eval_jaxpr/ppermute | solution.py:13
  332.0 2.0 multiply_reduce_fusion.3
  337.1 6.4 %collective-permute-done = bf16[16,8192]{1,0:T(8,128)(2,1)S(1)} collective-permute-done((bf16[16,8192]{1,0:T(8,128)(2,1)}, bf16[16,8192]{1,0:T(8,128)(2,1)S(1)}, u32[]{:S(2)}, u32[]{:S(2)}) %collective-permute-start) | collective-permute-done | bytes 262176 | tf_op jit(solution)/shard_map/while/body/eval_jaxpr/ppermute | solution.py:13
  344.5 2.0 multiply_reduce_fusion.3
  349.6 7.0 %collective-permute-done = bf16[16,8192]{1,0:T(8,128)(2,1)S(1)} collective-permute-done((bf16[16,8192]{1,0:T(8,128)(2,1)}, bf16[16,8192]{1,0:T(8,128)(2,1)S(1)}, u32[]{:S(2)}, u32[]{:S(2)}) %collective-permute-start) | collective-permute-done | bytes 262176 | tf_op jit(solution)/shard_map/while/body/eval_jaxpr/ppermute | solution.py:13
  357.7 2.0 multiply_reduce_fusion.3
  362.8 7.2 %collective-permute-done = bf16[16,8192]{1,0:T(8,128)(2,1)S(1)} collective-permute-done((bf16[16,8192]{1,0:T(8,128)(2,1)}, bf16[16,8192]{1,0:T(8,128)(2,1)S(1)}, u32[]{:S(2)}, u32[]{:S(2)}) %collective-permute-start) | collective-permute-done | bytes 262176 | tf_op jit(solution)/shard_map/while/body/eval_jaxpr/ppermute | solution.py:13
  371.1 2.0 multiply_reduce_fusion.3
  376.2 7.2 %collective-permute-done = bf16[16,8192]{1,0:T(8,128)(2,1)S(1)} collective-permute-done((bf16[16,8192]{1,0:T(8,128)(2,1)}, bf16[16,8192]{1,0:T(8,128)(2,1)S(1)}, u32[]{:S(2)}, u32[]{:S(2)}) %collective-permute-start) | collective-permute-done | bytes 262176 | tf_op jit(solution)/shard_map/while/body/eval_jaxpr/ppermute | solution.py:13
  389.7 7.2 %collective-permute-done = bf16[16,8192]{1,0:T(8,128)(2,1)S(1)} collective-permute-done((bf16[16,8192]{1,0:T(8,128)(2,1)}, bf16[16,8192]{1,0:T(8,128)(2,1)S(1)}, u32[]{:S(2)}, u32[]{:S(2)}) %collective-permute-start) | collective-permute-done | bytes 262176 | tf_op jit(solution)/shard_map/while/body/eval_jaxpr/ppermute | solution.py:13
  402.1 4.3 fusion.3
  406.4 2.5 fusion.2
  410.6 65.9 %reduce-scatter.2.cloned.1.call-done = f32[65,1024]{1,0:T(8,128)} async-done(((f32[65,8192]{1,0:T(8,128)}), f32[65,1024]{1,0:T(8,128)}) %reduce-scatter.2.cloned.1.call-update) | async-done | bytes 266256 | tf_op jit(solution)/shard_map/reduce_scatter | solution.py:89
  478.8 106.0 %psum.7 = f32[4]{0:T(128)S(1)} all-reduce(f32[4]{0:T(128)S(1)} %compare_select_fusion), channel_id=1, replica_groups=mesh['pipe'=16,'seq'=8,'dp'=4] {'pipe','seq','dp'}, use_global_device_ids=true, to_apply=%region_7.8 | all-reduce | flops 4 | bytes 32 | tf_op jit(solution)/shard_map/psum | solution.py:94
  (160 shorter events, 123.6 us)
Async XLA Ops:
  7.2 67.9 %all-gather.5.cloned.1.call-start = ((), (), s32[]{:S(2)}) async-start(), calls=%async_computation.1 | async-start | bytes 1216512 | tf_op jit(solution)/shard_map/all_gather | solution.py:23
  8.6 467.8 %reduce-scatter.2.cloned.1.call-start = ((), (), s32[]{:S(2)}) async-start(), calls=%async_computation.2 | async-start | bytes 2654208 | tf_op jit(solution)/shard_map/reduce_scatter | solution.py:89
  83.4 9.7 %collective-permute-start = (bf16[16,8192]{1,0:T(8,128)(2,1)}, bf16[16,8192]{1,0:T(8,128)(2,1)S(1)}, u32[]{:S(2)}, u32[]{:S(2)}) collective-permute-start(bf16[16,8192]{1,0:T(8,128)(2,1)} %add_convert_fusion.2), channel_id=1, source_target_pairs={{32,0},{64,32},{96,64},{128,96},{160,128},{192,160},{224,192},{256... | collective-permute-start | bytes 786440 | tf_op jit(solution)/shard_map/while/body/eval_jaxpr/ppermute | solution.py:13
  98.0 8.8 %collective-permute-start = (bf16[16,8192]{1,0:T(8,128)(2,1)}, bf16[16,8192]{1,0:T(8,128)(2,1)S(1)}, u32[]{:S(2)}, u32[]{:S(2)}) collective-permute-start(bf16[16,8192]{1,0:T(8,128)(2,1)} %add_convert_fusion.2), channel_id=1, source_target_pairs={{32,0},{64,32},{96,64},{128,96},{160,128},{192,160},{224,192},{256... | collective-permute-start | bytes 786440 | tf_op jit(solution)/shard_map/while/body/eval_jaxpr/ppermute | solution.py:13
  111.7 8.0 %collective-permute-start = (bf16[16,8192]{1,0:T(8,128)(2,1)}, bf16[16,8192]{1,0:T(8,128)(2,1)S(1)}, u32[]{:S(2)}, u32[]{:S(2)}) collective-permute-start(bf16[16,8192]{1,0:T(8,128)(2,1)} %add_convert_fusion.2), channel_id=1, source_target_pairs={{32,0},{64,32},{96,64},{128,96},{160,128},{192,160},{224,192},{256... | collective-permute-start | bytes 786440 | tf_op jit(solution)/shard_map/while/body/eval_jaxpr/ppermute | solution.py:13
  124.6 9.5 %collective-permute-start = (bf16[16,8192]{1,0:T(8,128)(2,1)}, bf16[16,8192]{1,0:T(8,128)(2,1)S(1)}, u32[]{:S(2)}, u32[]{:S(2)}) collective-permute-start(bf16[16,8192]{1,0:T(8,128)(2,1)} %add_convert_fusion.2), channel_id=1, source_target_pairs={{32,0},{64,32},{96,64},{128,96},{160,128},{192,160},{224,192},{256... | collective-permute-start | bytes 786440 | tf_op jit(solution)/shard_map/while/body/eval_jaxpr/ppermute | solution.py:13
  139.0 7.7 %collective-permute-start = (bf16[16,8192]{1,0:T(8,128)(2,1)}, bf16[16,8192]{1,0:T(8,128)(2,1)S(1)}, u32[]{:S(2)}, u32[]{:S(2)}) collective-permute-start(bf16[16,8192]{1,0:T(8,128)(2,1)} %add_convert_fusion.2), channel_id=1, source_target_pairs={{32,0},{64,32},{96,64},{128,96},{160,128},{192,160},{224,192},{256... | collective-permute-start | bytes 786440 | tf_op jit(solution)/shard_map/while/body/eval_jaxpr/ppermute | solution.py:13
  151.6 7.9 %collective-permute-start = (bf16[16,8192]{1,0:T(8,128)(2,1)}, bf16[16,8192]{1,0:T(8,128)(2,1)S(1)}, u32[]{:S(2)}, u32[]{:S(2)}) collective-permute-start(bf16[16,8192]{1,0:T(8,128)(2,1)} %add_convert_fusion.2), channel_id=1, source_target_pairs={{32,0},{64,32},{96,64},{128,96},{160,128},{192,160},{224,192},{256... | collective-permute-start | bytes 786440 | tf_op jit(solution)/shard_map/while/body/eval_jaxpr/ppermute | solution.py:13
  164.4 8.5 %collective-permute-start = (bf16[16,8192]{1,0:T(8,128)(2,1)}, bf16[16,8192]{1,0:T(8,128)(2,1)S(1)}, u32[]{:S(2)}, u32[]{:S(2)}) collective-permute-start(bf16[16,8192]{1,0:T(8,128)(2,1)} %add_convert_fusion.2), channel_id=1, source_target_pairs={{32,0},{64,32},{96,64},{128,96},{160,128},{192,160},{224,192},{256... | collective-permute-start | bytes 786440 | tf_op jit(solution)/shard_map/while/body/eval_jaxpr/ppermute | solution.py:13
  177.8 8.5 %collective-permute-start = (bf16[16,8192]{1,0:T(8,128)(2,1)}, bf16[16,8192]{1,0:T(8,128)(2,1)S(1)}, u32[]{:S(2)}, u32[]{:S(2)}) collective-permute-start(bf16[16,8192]{1,0:T(8,128)(2,1)} %add_convert_fusion.2), channel_id=1, source_target_pairs={{32,0},{64,32},{96,64},{128,96},{160,128},{192,160},{224,192},{256... | collective-permute-start | bytes 786440 | tf_op jit(solution)/shard_map/while/body/eval_jaxpr/ppermute | solution.py:13
  191.2 8.5 %collective-permute-start = (bf16[16,8192]{1,0:T(8,128)(2,1)}, bf16[16,8192]{1,0:T(8,128)(2,1)S(1)}, u32[]{:S(2)}, u32[]{:S(2)}) collective-permute-start(bf16[16,8192]{1,0:T(8,128)(2,1)} %add_convert_fusion.2), channel_id=1, source_target_pairs={{32,0},{64,32},{96,64},{128,96},{160,128},{192,160},{224,192},{256... | collective-permute-start | bytes 786440 | tf_op jit(solution)/shard_map/while/body/eval_jaxpr/ppermute | solution.py:13
  204.7 8.5 %collective-permute-start = (bf16[16,8192]{1,0:T(8,128)(2,1)}, bf16[16,8192]{1,0:T(8,128)(2,1)S(1)}, u32[]{:S(2)}, u32[]{:S(2)}) collective-permute-start(bf16[16,8192]{1,0:T(8,128)(2,1)} %add_convert_fusion.2), channel_id=1, source_target_pairs={{32,0},{64,32},{96,64},{128,96},{160,128},{192,160},{224,192},{256... | collective-permute-start | bytes 786440 | tf_op jit(solution)/shard_map/while/body/eval_jaxpr/ppermute | solution.py:13
  218.1 8.5 %collective-permute-start = (bf16[16,8192]{1,0:T(8,128)(2,1)}, bf16[16,8192]{1,0:T(8,128)(2,1)S(1)}, u32[]{:S(2)}, u32[]{:S(2)}) collective-permute-start(bf16[16,8192]{1,0:T(8,128)(2,1)} %add_convert_fusion.2), channel_id=1, source_target_pairs={{32,0},{64,32},{96,64},{128,96},{160,128},{192,160},{224,192},{256... | collective-permute-start | bytes 786440 | tf_op jit(solution)/shard_map/while/body/eval_jaxpr/ppermute | solution.py:13
  231.6 8.5 %collective-permute-start = (bf16[16,8192]{1,0:T(8,128)(2,1)}, bf16[16,8192]{1,0:T(8,128)(2,1)S(1)}, u32[]{:S(2)}, u32[]{:S(2)}) collective-permute-start(bf16[16,8192]{1,0:T(8,128)(2,1)} %add_convert_fusion.2), channel_id=1, source_target_pairs={{32,0},{64,32},{96,64},{128,96},{160,128},{192,160},{224,192},{256... | collective-permute-start | bytes 786440 | tf_op jit(solution)/shard_map/while/body/eval_jaxpr/ppermute | solution.py:13
  245.0 9.7 %collective-permute-start = (bf16[16,8192]{1,0:T(8,128)(2,1)}, bf16[16,8192]{1,0:T(8,128)(2,1)S(1)}, u32[]{:S(2)}, u32[]{:S(2)}) collective-permute-start(bf16[16,8192]{1,0:T(8,128)(2,1)} %add_convert_fusion.2), channel_id=1, source_target_pairs={{32,0},{64,32},{96,64},{128,96},{160,128},{192,160},{224,192},{256... | collective-permute-start | bytes 786440 | tf_op jit(solution)/shard_map/while/body/eval_jaxpr/ppermute | solution.py:13
  259.6 11.3 %collective-permute-start = (bf16[16,8192]{1,0:T(8,128)(2,1)}, bf16[16,8192]{1,0:T(8,128)(2,1)S(1)}, u32[]{:S(2)}, u32[]{:S(2)}) collective-permute-start(bf16[16,8192]{1,0:T(8,128)(2,1)} %add_convert_fusion.2), channel_id=1, source_target_pairs={{32,0},{64,32},{96,64},{128,96},{160,128},{192,160},{224,192},{256... | collective-permute-start | bytes 786440 | tf_op jit(solution)/shard_map/while/body/eval_jaxpr/ppermute | solution.py:13
  275.8 11.9 %collective-permute-start = (bf16[16,8192]{1,0:T(8,128)(2,1)}, bf16[16,8192]{1,0:T(8,128)(2,1)S(1)}, u32[]{:S(2)}, u32[]{:S(2)}) collective-permute-start(bf16[16,8192]{1,0:T(8,128)(2,1)} %add_convert_fusion.2), channel_id=1, source_target_pairs={{32,0},{64,32},{96,64},{128,96},{160,128},{192,160},{224,192},{256... | collective-permute-start | bytes 786440 | tf_op jit(solution)/shard_map/while/body/eval_jaxpr/ppermute | solution.py:13
  292.7 11.2 %collective-permute-start = (bf16[16,8192]{1,0:T(8,128)(2,1)}, bf16[16,8192]{1,0:T(8,128)(2,1)S(1)}, u32[]{:S(2)}, u32[]{:S(2)}) collective-permute-start(bf16[16,8192]{1,0:T(8,128)(2,1)} %add_convert_fusion.2), channel_id=1, source_target_pairs={{32,0},{64,32},{96,64},{128,96},{160,128},{192,160},{224,192},{256... | collective-permute-start | bytes 786440 | tf_op jit(solution)/shard_map/while/body/eval_jaxpr/ppermute | solution.py:13
  308.8 9.2 %collective-permute-start = (bf16[16,8192]{1,0:T(8,128)(2,1)}, bf16[16,8192]{1,0:T(8,128)(2,1)S(1)}, u32[]{:S(2)}, u32[]{:S(2)}) collective-permute-start(bf16[16,8192]{1,0:T(8,128)(2,1)} %add_convert_fusion.2), channel_id=1, source_target_pairs={{32,0},{64,32},{96,64},{128,96},{160,128},{192,160},{224,192},{256... | collective-permute-start | bytes 786440 | tf_op jit(solution)/shard_map/while/body/eval_jaxpr/ppermute | solution.py:13
  322.9 8.0 %collective-permute-start = (bf16[16,8192]{1,0:T(8,128)(2,1)}, bf16[16,8192]{1,0:T(8,128)(2,1)S(1)}, u32[]{:S(2)}, u32[]{:S(2)}) collective-permute-start(bf16[16,8192]{1,0:T(8,128)(2,1)} %add_convert_fusion.2), channel_id=1, source_target_pairs={{32,0},{64,32},{96,64},{128,96},{160,128},{192,160},{224,192},{256... | collective-permute-start | bytes 786440 | tf_op jit(solution)/shard_map/while/body/eval_jaxpr/ppermute | solution.py:13
  335.8 7.7 %collective-permute-start = (bf16[16,8192]{1,0:T(8,128)(2,1)}, bf16[16,8192]{1,0:T(8,128)(2,1)S(1)}, u32[]{:S(2)}, u32[]{:S(2)}) collective-permute-start(bf16[16,8192]{1,0:T(8,128)(2,1)} %add_convert_fusion.2), channel_id=1, source_target_pairs={{32,0},{64,32},{96,64},{128,96},{160,128},{192,160},{224,192},{256... | collective-permute-start | bytes 786440 | tf_op jit(solution)/shard_map/while/body/eval_jaxpr/ppermute | solution.py:13
  348.4 8.2 %collective-permute-start = (bf16[16,8192]{1,0:T(8,128)(2,1)}, bf16[16,8192]{1,0:T(8,128)(2,1)S(1)}, u32[]{:S(2)}, u32[]{:S(2)}) collective-permute-start(bf16[16,8192]{1,0:T(8,128)(2,1)} %add_convert_fusion.2), channel_id=1, source_target_pairs={{32,0},{64,32},{96,64},{128,96},{160,128},{192,160},{224,192},{256... | collective-permute-start | bytes 786440 | tf_op jit(solution)/shard_map/while/body/eval_jaxpr/ppermute | solution.py:13
  361.5 8.5 %collective-permute-start = (bf16[16,8192]{1,0:T(8,128)(2,1)}, bf16[16,8192]{1,0:T(8,128)(2,1)S(1)}, u32[]{:S(2)}, u32[]{:S(2)}) collective-permute-start(bf16[16,8192]{1,0:T(8,128)(2,1)} %add_convert_fusion.2), channel_id=1, source_target_pairs={{32,0},{64,32},{96,64},{128,96},{160,128},{192,160},{224,192},{256... | collective-permute-start | bytes 786440 | tf_op jit(solution)/shard_map/while/body/eval_jaxpr/ppermute | solution.py:13
  374.9 8.5 %collective-permute-start = (bf16[16,8192]{1,0:T(8,128)(2,1)}, bf16[16,8192]{1,0:T(8,128)(2,1)S(1)}, u32[]{:S(2)}, u32[]{:S(2)}) collective-permute-start(bf16[16,8192]{1,0:T(8,128)(2,1)} %add_convert_fusion.2), channel_id=1, source_target_pairs={{32,0},{64,32},{96,64},{128,96},{160,128},{192,160},{224,192},{256... | collective-permute-start | bytes 786440 | tf_op jit(solution)/shard_map/while/body/eval_jaxpr/ppermute | solution.py:13
  388.4 8.5 %collective-permute-start = (bf16[16,8192]{1,0:T(8,128)(2,1)}, bf16[16,8192]{1,0:T(8,128)(2,1)S(1)}, u32[]{:S(2)}, u32[]{:S(2)}) collective-permute-start(bf16[16,8192]{1,0:T(8,128)(2,1)} %add_convert_fusion.2), channel_id=1, source_target_pairs={{32,0},{64,32},{96,64},{128,96},{160,128},{192,160},{224,192},{256... | collective-permute-start | bytes 786440 | tf_op jit(solution)/shard_map/while/body/eval_jaxpr/ppermute | solution.py:13
  396.9 0.6 copy-start.6
  397.5 1.7 copy-start.3
  397.7 1.3 copy-start
  397.7 2.5 copy-start.2
  397.7 2.5 copy-start.7
  400.2 1.8 copy-start.1
  406.3 2.5 copy-start.4
  406.3 2.5 copy-start.5
  410.5 174.8 %all-gather.7.cloned.1.call-start = ((), (), s32[]{:S(2)}) async-start(), calls=%async_computation.3 | async-start | bytes 1474560 | tf_op jit(solution)/shard_map/all_gather | solution.py:97
Sparse Core Ops, SparseCore 0:
  11.0 63.9 all-gather.4
  410.7 65.7 reduce-scatter.1
  478.6 31.4 all-gather.6
where the time goes:
time: 597 us; the launch traced here: 594 us
  waiting for transfers between devices  306 us (51%)
  blocking collectives  106 us (18%)
  other arithmetic  75.5 us (13%)
  matrix products  54.4 us (9%)
  starting transfers between devices  29.6 us (5%)
  between operations  13.9 us (2%)
  local copies, waits for them, and re-layouts  8.42 us (1%)
    ppermute x23, waiting for transfers between devices, from_behind(): lax.ppermute(value, axis, [(source, source + steps) for source in range(i...  176 us
    psum x1, blocking collectives, on_device(): totals = lax.psum(squares, ('pipe', 'seq', 'dp'))  106 us
    reduce_scatter x1, waiting for transfers between devices, on_device(): part = lax.psum_scatter(grads, 'seq', scatter_dimension=1, tiled=True)  65.9 us
    all_gather x1, waiting for transfers between devices, on_device(): whole = lax.all_gather(params, ('seq', 'dp'), axis=1, tiled=True)  64.3 us
    dot_general x23, matrix products, back_block(): jnp.dot(d_low, a_full, preferred_element_type=jnp.float32)  44.9 us
    convert_element_type x23, other arithmetic, back_block(): return hidden_gradient.astype(jnp.bfloat16)  42.7 us
    ppermute x23, starting transfers between devices, from_behind(): lax.ppermute(value, axis, [(source, source + steps) for source in range(i...  29.4 us
    dynamic_update_slice x23, other arithmetic, turn(): store = lax.dynamic_update_slice_in_dim(store, source[None], slot, 0)  23.3 us
  transfers between devices with their start and end apart: 26, of which 25 were waited for; matrix products, arithmetic and copies ran while one was open for 1% of the time, Pallas kernels for 0%

commit v1 on v0

--- a/solution.py
+++ b/solution.py
@@ -1,3 +1,4 @@
+import functools
 import math
 import jax
 import jax.numpy as jnp
@@ -5,6 +6,14 @@
 from jax.sharding import PartitionSpec as P
 
 rows_per_block = 16
+
+
+def step_on_point(x0, ndim_at):
+    g_now = jnp.concatenate([x0 for _ in range(lax.psum(1, ("seq", "dp")))], axis=ndim_at)
+    return lax.all_to_all(g_now, ("seq", "dp"), ndim_at, ndim_at, tiled=True)
+
+
+map_sheet = functools.partial(step_on_point, ndim_at=1)
 
 
 def from_behind(value, axis, steps):
@@ -20,7 +29,7 @@
     top = top_grad[0]
     rank = a_rows.shape[1]
     params = jnp.concatenate([a_rows[0], b_rows[0], gain], axis=0)
-    whole = lax.all_gather(params, ("seq", "dp"), axis=1, tiled=True)
+    whole = map_sheet(params)
     a_full = whole[:rank]
     b_full = whole[rank : 2 * rank]
     gain_float = whole[2 * rank].astype(jnp.float32)

time: 597 us -> 570 us (0.955)
  waiting for transfers between devices: 306 us -> 260 us
  starting transfers between devices: 29.6 us -> 40.1 us
  other arithmetic: 75.5 us -> 84.4 us
    all_gather x1 -> x0, waiting for transfers between devices: 64.3 us -> none  [on_device(): whole = lax.all_gather(params, ('seq', 'dp'), axis=1, tiled=True)]
    all_to_all x0 -> x1, waiting for transfers between devices: none -> 16.8 us  [step_on_point(): return lax.all_to_all(g_now, ('seq', 'dp'), ndim_at, ndim_at, tiled=True)]
    unnamed x0 -> x31, other arithmetic: none -> 13 us
    all_to_all x0 -> x1, starting transfers between devices: none -> 10.6 us  [step_on_point(): return lax.all_to_all(g_now, ('seq', 'dp'), ndim_at, ndim_at, tiled=True)]
where the time goes in v1:
time: 570 us; the launch traced here: 566 us
  waiting for transfers between devices  260 us (46%)
  blocking collectives  106 us (19%)
  other arithmetic  84.4 us (15%)
  matrix products  50.8 us (9%)
  starting transfers between devices  40.1 us (7%)
  between operations  14.3 us (3%)
  local copies, waits for them, and re-layouts  9.5 us (2%)
    ppermute x23, waiting for transfers between devices, from_behind(): lax.ppermute(value, axis, [(source, source + steps) for source in range(i...  173 us
    psum x1, blocking collectives, on_device(): totals = lax.psum(squares, ('pipe', 'seq', 'dp'))  106 us
    reduce_scatter x1, waiting for transfers between devices, on_device(): part = lax.psum_scatter(grads, 'seq', scatter_dimension=1, tiled=True)  70.7 us
    dot_general x23, matrix products, back_block(): jnp.dot(d_low, a_full, preferred_element_type=jnp.float32)  44.9 us
    convert_element_type x23, other arithmetic, back_block(): return hidden_gradient.astype(jnp.bfloat16)  42.5 us
    ppermute x23, starting transfers between devices, from_behind(): lax.ppermute(value, axis, [(source, source + steps) for source in range(i...  29.4 us
    dynamic_update_slice x23, other arithmetic, turn(): store = lax.dynamic_update_slice_in_dim(store, source[None], slot, 0)  23.3 us
    all_to_all x1, waiting for transfers between devices, step_on_point(): return lax.all_to_all(g_now, ('seq', 'dp'), ndim_at, ndim_at, tiled=True)  16.8 us
  transfers between devices with their start and end apart: 26, of which 25 were waited for; matrix products, arithmetic and copies ran while one was open for 1% of the time, Pallas kernels for 0%

profile of v1, /device:TPU:1, one launch (start us, length us, event | category | flops | bytes accessed | tf_op | source)
XLA Modules:
  0.0 566.1 jit_solution(4059780460185855338)
XLA Ops:
  22.3 10.6 %all-to-all-start = ((bf16[65,32,256]{2,0,1:T(8,128)(2,1)}), bf16[65,32,256]{2,0,1:T(8,128)(2,1)S(1)}, u32[]{:S(2)}, u32[]{:S(2)}) async-start(bf16[65,32,256]{2,0,1:T(8,128)(2,1)} %copy.9), calls=%async_computation | async-start | bytes 2359296 | tf_op jit(solution)/shard_map/all_to_all | solution.py:13
  33.5 16.8 %all-to-all-done = bf16[65,32,256]{2,0,1:T(8,128)(2,1)S(1)} async-done(((bf16[65,32,256]{2,0,1:T(8,128)(2,1)}), bf16[65,32,256]{2,0,1:T(8,128)(2,1)S(1)}, u32[]{:S(2)}, u32[]{:S(2)}) %all-to-all-start) | async-done | bytes 1064992 | tf_op jit(solution)/shard_map/all_to_all | solution.py:13
  52.4 315.4 %while.17 = (s32[]{:T(128)}, bf16[16,8192]{1,0:T(8,128)(2,1)S(1)}, bf16[9,16,8192]{2,1,0:T(8,128)(2,1)S(1)}, pred[]{:T(512)}, s32[]{:T(128)}, /*index=5*/bf16[12...) while((s32[]{:T(128)}, bf16[16,8192]{1,0:T(8,128)(2,1)S(1)}, ...), condition=%wide.region_3.4_spmd, body=%wide.region_1.3_spmd.sunk | while | flops 18612752 | bytes 5538680 | solution.py:86
  58.7 7.4 %collective-permute-done = bf16[16,8192]{1,0:T(8,128)(2,1)S(1)} collective-permute-done((bf16[16,8192]{1,0:T(8,128)(2,1)}, bf16[16,8192]{1,0:T(8,128)(2,1)S(1)}, u32[]{:S(2)}, u32[]{:S(2)}) %collective-permute-start) | collective-permute-done | bytes 262176 | tf_op jit(solution)/shard_map/while/body/eval_jaxpr/ppermute | solution.py:22
  72.2 6.5 %collective-permute-done = bf16[16,8192]{1,0:T(8,128)(2,1)S(1)} collective-permute-done((bf16[16,8192]{1,0:T(8,128)(2,1)}, bf16[16,8192]{1,0:T(8,128)(2,1)S(1)}, u32[]{:S(2)}, u32[]{:S(2)}) %collective-permute-start) | collective-permute-done | bytes 262176 | tf_op jit(solution)/shard_map/while/body/eval_jaxpr/ppermute | solution.py:22
  79.9 2.0 multiply_reduce_fusion.3
  85.0 6.0 %collective-permute-done = bf16[16,8192]{1,0:T(8,128)(2,1)S(1)} collective-permute-done((bf16[16,8192]{1,0:T(8,128)(2,1)}, bf16[16,8192]{1,0:T(8,128)(2,1)S(1)}, u32[]{:S(2)}, u32[]{:S(2)}) %collective-permute-start) | collective-permute-done | bytes 262176 | tf_op jit(solution)/shard_map/while/body/eval_jaxpr/ppermute | solution.py:22
  97.2 7.2 %collective-permute-done = bf16[16,8192]{1,0:T(8,128)(2,1)S(1)} collective-permute-done((bf16[16,8192]{1,0:T(8,128)(2,1)}, bf16[16,8192]{1,0:T(8,128)(2,1)S(1)}, u32[]{:S(2)}, u32[]{:S(2)}) %collective-permute-start) | collective-permute-done | bytes 262176 | tf_op jit(solution)/shard_map/while/body/eval_jaxpr/ppermute | solution.py:22
  105.4 2.0 multiply_reduce_fusion.3
  110.5 6.5 %collective-permute-done = bf16[16,8192]{1,0:T(8,128)(2,1)S(1)} collective-permute-done((bf16[16,8192]{1,0:T(8,128)(2,1)}, bf16[16,8192]{1,0:T(8,128)(2,1)S(1)}, u32[]{:S(2)}, u32[]{:S(2)}) %collective-permute-start) | collective-permute-done | bytes 262176 | tf_op jit(solution)/shard_map/while/body/eval_jaxpr/ppermute | solution.py:22
  118.1 2.0 multiply_reduce_fusion.3
  123.3 7.2 %collective-permute-done = bf16[16,8192]{1,0:T(8,128)(2,1)S(1)} collective-permute-done((bf16[16,8192]{1,0:T(8,128)(2,1)}, bf16[16,8192]{1,0:T(8,128)(2,1)S(1)}, u32[]{:S(2)}, u32[]{:S(2)}) %collective-permute-start) | collective-permute-done | bytes 262176 | tf_op jit(solution)/shard_map/while/body/eval_jaxpr/ppermute | solution.py:22
  131.6 2.0 multiply_reduce_fusion.3
  136.7 7.2 %collective-permute-done = bf16[16,8192]{1,0:T(8,128)(2,1)S(1)} collective-permute-done((bf16[16,8192]{1,0:T(8,128)(2,1)}, bf16[16,8192]{1,0:T(8,128)(2,1)S(1)}, u32[]{:S(2)}, u32[]{:S(2)}) %collective-permute-start) | collective-permute-done | bytes 262176 | tf_op jit(solution)/shard_map/while/body/eval_jaxpr/ppermute | solution.py:22
  145.0 2.0 multiply_reduce_fusion.3
  150.1 7.2 %collective-permute-done = bf16[16,8192]{1,0:T(8,128)(2,1)S(1)} collective-permute-done((bf16[16,8192]{1,0:T(8,128)(2,1)}, bf16[16,8192]{1,0:T(8,128)(2,1)S(1)}, u32[]{:S(2)}, u32[]{:S(2)}) %collective-permute-start) | collective-permute-done | bytes 262176 | tf_op jit(solution)/shard_map/while/body/eval_jaxpr/ppermute | solution.py:22
  158.4 2.0 multiply_reduce_fusion.3
  163.5 7.2 %collective-permute-done = bf16[16,8192]{1,0:T(8,128)(2,1)S(1)} collective-permute-done((bf16[16,8192]{1,0:T(8,128)(2,1)}, bf16[16,8192]{1,0:T(8,128)(2,1)S(1)}, u32[]{:S(2)}, u32[]{:S(2)}) %collective-permute-start) | collective-permute-done | bytes 262176 | tf_op jit(solution)/shard_map/while/body/eval_jaxpr/ppermute | solution.py:22
  171.8 2.0 multiply_reduce_fusion.3
  176.9 7.2 %collective-permute-done = bf16[16,8192]{1,0:T(8,128)(2,1)S(1)} collective-permute-done((bf16[16,8192]{1,0:T(8,128)(2,1)}, bf16[16,8192]{1,0:T(8,128)(2,1)S(1)}, u32[]{:S(2)}, u32[]{:S(2)}) %collective-permute-start) | collective-permute-done | bytes 262176 | tf_op jit(solution)/shard_map/while/body/eval_jaxpr/ppermute | solution.py:22
  185.3 2.0 multiply_reduce_fusion.3
  190.4 7.2 %collective-permute-done = bf16[16,8192]{1,0:T(8,128)(2,1)S(1)} collective-permute-done((bf16[16,8192]{1,0:T(8,128)(2,1)}, bf16[16,8192]{1,0:T(8,128)(2,1)S(1)}, u32[]{:S(2)}, u32[]{:S(2)}) %collective-permute-start) | collective-permute-done | bytes 262176 | tf_op jit(solution)/shard_map/while/body/eval_jaxpr/ppermute | solution.py:22
  198.7 2.0 multiply_reduce_fusion.3
  203.8 8.3 %collective-permute-done = bf16[16,8192]{1,0:T(8,128)(2,1)S(1)} collective-permute-done((bf16[16,8192]{1,0:T(8,128)(2,1)}, bf16[16,8192]{1,0:T(8,128)(2,1)S(1)}, u32[]{:S(2)}, u32[]{:S(2)}) %collective-permute-start) | collective-permute-done | bytes 262176 | tf_op jit(solution)/shard_map/while/body/eval_jaxpr/ppermute | solution.py:22
  213.2 2.0 multiply_reduce_fusion.3
  218.3 9.9 %collective-permute-done = bf16[16,8192]{1,0:T(8,128)(2,1)S(1)} collective-permute-done((bf16[16,8192]{1,0:T(8,128)(2,1)}, bf16[16,8192]{1,0:T(8,128)(2,1)S(1)}, u32[]{:S(2)}, u32[]{:S(2)}) %collective-permute-start) | collective-permute-done | bytes 262176 | tf_op jit(solution)/shard_map/while/body/eval_jaxpr/ppermute | solution.py:22
  229.3 2.0 multiply_reduce_fusion.3
  234.4 10.7 %collective-permute-done = bf16[16,8192]{1,0:T(8,128)(2,1)S(1)} collective-permute-done((bf16[16,8192]{1,0:T(8,128)(2,1)}, bf16[16,8192]{1,0:T(8,128)(2,1)S(1)}, u32[]{:S(2)}, u32[]{:S(2)}) %collective-permute-start) | collective-permute-done | bytes 262176 | tf_op jit(solution)/shard_map/while/body/eval_jaxpr/ppermute | solution.py:22
  246.2 2.0 multiply_reduce_fusion.3
  251.3 9.8 %collective-permute-done = bf16[16,8192]{1,0:T(8,128)(2,1)S(1)} collective-permute-done((bf16[16,8192]{1,0:T(8,128)(2,1)}, bf16[16,8192]{1,0:T(8,128)(2,1)S(1)}, u32[]{:S(2)}, u32[]{:S(2)}) %collective-permute-start) | collective-permute-done | bytes 262176 | tf_op jit(solution)/shard_map/while/body/eval_jaxpr/ppermute | solution.py:22
  262.2 2.0 multiply_reduce_fusion.3
  267.3 8.3 %collective-permute-done = bf16[16,8192]{1,0:T(8,128)(2,1)S(1)} collective-permute-done((bf16[16,8192]{1,0:T(8,128)(2,1)}, bf16[16,8192]{1,0:T(8,128)(2,1)S(1)}, u32[]{:S(2)}, u32[]{:S(2)}) %collective-permute-start) | collective-permute-done | bytes 262176 | tf_op jit(solution)/shard_map/while/body/eval_jaxpr/ppermute | solution.py:22
  276.6 2.0 multiply_reduce_fusion.3
  281.7 6.7 %collective-permute-done = bf16[16,8192]{1,0:T(8,128)(2,1)S(1)} collective-permute-done((bf16[16,8192]{1,0:T(8,128)(2,1)}, bf16[16,8192]{1,0:T(8,128)(2,1)S(1)}, u32[]{:S(2)}, u32[]{:S(2)}) %collective-permute-start) | collective-permute-done | bytes 262176 | tf_op jit(solution)/shard_map/while/body/eval_jaxpr/ppermute | solution.py:22
  294.6 6.3 %collective-permute-done = bf16[16,8192]{1,0:T(8,128)(2,1)S(1)} collective-permute-done((bf16[16,8192]{1,0:T(8,128)(2,1)}, bf16[16,8192]{1,0:T(8,128)(2,1)S(1)}, u32[]{:S(2)}, u32[]{:S(2)}) %collective-permute-start) | collective-permute-done | bytes 262176 | tf_op jit(solution)/shard_map/while/body/eval_jaxpr/ppermute | solution.py:22
  302.0 2.0 multiply_reduce_fusion.3
  307.2 7.0 %collective-permute-done = bf16[16,8192]{1,0:T(8,128)(2,1)S(1)} collective-permute-done((bf16[16,8192]{1,0:T(8,128)(2,1)}, bf16[16,8192]{1,0:T(8,128)(2,1)S(1)}, u32[]{:S(2)}, u32[]{:S(2)}) %collective-permute-start) | collective-permute-done | bytes 262176 | tf_op jit(solution)/shard_map/while/body/eval_jaxpr/ppermute | solution.py:22
  315.2 2.0 multiply_reduce_fusion.3
  320.3 7.2 %collective-permute-done = bf16[16,8192]{1,0:T(8,128)(2,1)S(1)} collective-permute-done((bf16[16,8192]{1,0:T(8,128)(2,1)}, bf16[16,8192]{1,0:T(8,128)(2,1)S(1)}, u32[]{:S(2)}, u32[]{:S(2)}) %collective-permute-start) | collective-permute-done | bytes 262176 | tf_op jit(solution)/shard_map/while/body/eval_jaxpr/ppermute | solution.py:22
  328.6 2.0 multiply_reduce_fusion.3
  333.7 7.2 %collective-permute-done = bf16[16,8192]{1,0:T(8,128)(2,1)S(1)} collective-permute-done((bf16[16,8192]{1,0:T(8,128)(2,1)}, bf16[16,8192]{1,0:T(8,128)(2,1)S(1)}, u32[]{:S(2)}, u32[]{:S(2)}) %collective-permute-start) | collective-permute-done | bytes 262176 | tf_op jit(solution)/shard_map/while/body/eval_jaxpr/ppermute | solution.py:22
  342.0 2.0 multiply_reduce_fusion.3
  347.1 7.2 %collective-permute-done = bf16[16,8192]{1,0:T(8,128)(2,1)S(1)} collective-permute-done((bf16[16,8192]{1,0:T(8,128)(2,1)}, bf16[16,8192]{1,0:T(8,128)(2,1)S(1)}, u32[]{:S(2)}, u32[]{:S(2)}) %collective-permute-start) | collective-permute-done | bytes 262176 | tf_op jit(solution)/shard_map/while/body/eval_jaxpr/ppermute | solution.py:22
  355.5 2.0 multiply_reduce_fusion.3
  360.6 7.2 %collective-permute-done = bf16[16,8192]{1,0:T(8,128)(2,1)S(1)} collective-permute-done((bf16[16,8192]{1,0:T(8,128)(2,1)}, bf16[16,8192]{1,0:T(8,128)(2,1)S(1)}, u32[]{:S(2)}, u32[]{:S(2)}) %collective-permute-start) | collective-permute-done | bytes 262176 | tf_op jit(solution)/shard_map/while/body/eval_jaxpr/ppermute | solution.py:22
  370.4 3.5 fusion.11
  377.4 70.7 %reduce-scatter.2.cloned.1.call-done = f32[65,1024]{1,0:T(8,128)} async-done(((f32[65,8192]{1,0:T(8,128)}), f32[65,1024]{1,0:T(8,128)}) %reduce-scatter.2.cloned.1.call-update) | async-done | bytes 266256 | tf_op jit(solution)/shard_map/reduce_scatter | solution.py:98
  450.4 106.0 %psum.7 = f32[4]{0:T(128)S(1)} all-reduce(f32[4]{0:T(128)S(1)} %compare_select_fusion), channel_id=1, replica_groups=mesh['pipe'=16,'seq'=8,'dp'=4] {'pipe','seq','dp'}, use_global_device_ids=true, to_apply=%region_7.8 | all-reduce | flops 4 | bytes 32 | tf_op jit(solution)/shard_map/psum | solution.py:103
  (195 shorter events, 133.7 us)
Async XLA Ops:
  7.2 12.9 %copy-start.1 = (bf16[1,32,256]{2,1,0:T(8,128)(2,1)S(1)}, bf16[1,32,256]{2,1,0:T(8,128)(2,1)}, u32[]{:S(2)}) copy-start(bf16[1,32,256]{2,1,0:T(8,128)(2,1)} %param.9) | copy-start | bytes 49156
  7.2 12.9 %copy-start = (bf16[1,32,256]{2,1,0:T(8,128)(2,1)S(1)}, bf16[1,32,256]{2,1,0:T(8,128)(2,1)}, u32[]{:S(2)}) copy-start(bf16[1,32,256]{2,1,0:T(8,128)(2,1)} %param.10) | copy-start | bytes 49156
  7.2 12.9 %copy-start.6 = (bf16[1,256]{1,0:T(2,128)(2,1)S(1)}, bf16[1,256]{1,0:T(2,128)(2,1)}, u32[]{:S(2)}) copy-start(bf16[1,256]{1,0:T(2,128)(2,1)} %param.11) | copy-start | bytes 1540
  22.3 10.6 %copy-start.3 = (bf16[1,1,128,8192]{3,2,1,0:T(8,128)(2,1)S(1)}, bf16[1,1,128,8192]{3,2,1,0:T(8,128)(2,1)}, u32[]{:S(2)}) copy-start(bf16[1,1,128,8192]{3,2,1,0:T(8,128)(2,1)} %param.7) | copy-start | bytes 6291460
  22.3 28.0 %all-to-all-start = ((bf16[65,32,256]{2,0,1:T(8,128)(2,1)}), bf16[65,32,256]{2,0,1:T(8,128)(2,1)S(1)}, u32[]{:S(2)}, u32[]{:S(2)}) async-start(bf16[65,32,256]{2,0,1:T(8,128)(2,1)} %copy.9), calls=%async_computation | async-start | bytes 2359296 | tf_op jit(solution)/shard_map/all_to_all | solution.py:13
  32.9 415.2 %reduce-scatter.2.cloned.1.call-start = ((), (), s32[]{:S(2)}) async-start(), calls=%async_computation.2 | async-start | bytes 2654208 | tf_op jit(solution)/shard_map/reduce_scatter | solution.py:98
  57.4 8.7 %collective-permute-start = (bf16[16,8192]{1,0:T(8,128)(2,1)}, bf16[16,8192]{1,0:T(8,128)(2,1)S(1)}, u32[]{:S(2)}, u32[]{:S(2)}) collective-permute-start(bf16[16,8192]{1,0:T(8,128)(2,1)} %add_convert_fusion.2), channel_id=1, source_target_pairs={{32,0},{64,32},{96,64},{128,96},{160,128},{192,160},{224,192},{256... | collective-permute-start | bytes 786440 | tf_op jit(solution)/shard_map/while/body/eval_jaxpr/ppermute | solution.py:22
  70.9 7.8 %collective-permute-start = (bf16[16,8192]{1,0:T(8,128)(2,1)}, bf16[16,8192]{1,0:T(8,128)(2,1)S(1)}, u32[]{:S(2)}, u32[]{:S(2)}) collective-permute-start(bf16[16,8192]{1,0:T(8,128)(2,1)} %add_convert_fusion.2), channel_id=1, source_target_pairs={{32,0},{64,32},{96,64},{128,96},{160,128},{192,160},{224,192},{256... | collective-permute-start | bytes 786440 | tf_op jit(solution)/shard_map/while/body/eval_jaxpr/ppermute | solution.py:22
  83.7 7.3 %collective-permute-start = (bf16[16,8192]{1,0:T(8,128)(2,1)}, bf16[16,8192]{1,0:T(8,128)(2,1)S(1)}, u32[]{:S(2)}, u32[]{:S(2)}) collective-permute-start(bf16[16,8192]{1,0:T(8,128)(2,1)} %add_convert_fusion.2), channel_id=1, source_target_pairs={{32,0},{64,32},{96,64},{128,96},{160,128},{192,160},{224,192},{256... | collective-permute-start | bytes 786440 | tf_op jit(solution)/shard_map/while/body/eval_jaxpr/ppermute | solution.py:22
  95.9 8.5 %collective-permute-start = (bf16[16,8192]{1,0:T(8,128)(2,1)}, bf16[16,8192]{1,0:T(8,128)(2,1)S(1)}, u32[]{:S(2)}, u32[]{:S(2)}) collective-permute-start(bf16[16,8192]{1,0:T(8,128)(2,1)} %add_convert_fusion.2), channel_id=1, source_target_pairs={{32,0},{64,32},{96,64},{128,96},{160,128},{192,160},{224,192},{256... | collective-permute-start | bytes 786440 | tf_op jit(solution)/shard_map/while/body/eval_jaxpr/ppermute | solution.py:22
  109.2 7.8 %collective-permute-start = (bf16[16,8192]{1,0:T(8,128)(2,1)}, bf16[16,8192]{1,0:T(8,128)(2,1)S(1)}, u32[]{:S(2)}, u32[]{:S(2)}) collective-permute-start(bf16[16,8192]{1,0:T(8,128)(2,1)} %add_convert_fusion.2), channel_id=1, source_target_pairs={{32,0},{64,32},{96,64},{128,96},{160,128},{192,160},{224,192},{256... | collective-permute-start | bytes 786440 | tf_op jit(solution)/shard_map/while/body/eval_jaxpr/ppermute | solution.py:22
  122.0 8.5 %collective-permute-start = (bf16[16,8192]{1,0:T(8,128)(2,1)}, bf16[16,8192]{1,0:T(8,128)(2,1)S(1)}, u32[]{:S(2)}, u32[]{:S(2)}) collective-permute-start(bf16[16,8192]{1,0:T(8,128)(2,1)} %add_convert_fusion.2), channel_id=1, source_target_pairs={{32,0},{64,32},{96,64},{128,96},{160,128},{192,160},{224,192},{256... | collective-permute-start | bytes 786440 | tf_op jit(solution)/shard_map/while/body/eval_jaxpr/ppermute | solution.py:22
  135.4 8.5 %collective-permute-start = (bf16[16,8192]{1,0:T(8,128)(2,1)}, bf16[16,8192]{1,0:T(8,128)(2,1)S(1)}, u32[]{:S(2)}, u32[]{:S(2)}) collective-permute-start(bf16[16,8192]{1,0:T(8,128)(2,1)} %add_convert_fusion.2), channel_id=1, source_target_pairs={{32,0},{64,32},{96,64},{128,96},{160,128},{192,160},{224,192},{256... | collective-permute-start | bytes 786440 | tf_op jit(solution)/shard_map/while/body/eval_jaxpr/ppermute | solution.py:22
  148.8 8.5 %collective-permute-start = (bf16[16,8192]{1,0:T(8,128)(2,1)}, bf16[16,8192]{1,0:T(8,128)(2,1)S(1)}, u32[]{:S(2)}, u32[]{:S(2)}) collective-permute-start(bf16[16,8192]{1,0:T(8,128)(2,1)} %add_convert_fusion.2), channel_id=1, source_target_pairs={{32,0},{64,32},{96,64},{128,96},{160,128},{192,160},{224,192},{256... | collective-permute-start | bytes 786440 | tf_op jit(solution)/shard_map/while/body/eval_jaxpr/ppermute | solution.py:22
  162.2 8.5 %collective-permute-start = (bf16[16,8192]{1,0:T(8,128)(2,1)}, bf16[16,8192]{1,0:T(8,128)(2,1)S(1)}, u32[]{:S(2)}, u32[]{:S(2)}) collective-permute-start(bf16[16,8192]{1,0:T(8,128)(2,1)} %add_convert_fusion.2), channel_id=1, source_target_pairs={{32,0},{64,32},{96,64},{128,96},{160,128},{192,160},{224,192},{256... | collective-permute-start | bytes 786440 | tf_op jit(solution)/shard_map/while/body/eval_jaxpr/ppermute | solution.py:22
  175.7 8.5 %collective-permute-start = (bf16[16,8192]{1,0:T(8,128)(2,1)}, bf16[16,8192]{1,0:T(8,128)(2,1)S(1)}, u32[]{:S(2)}, u32[]{:S(2)}) collective-permute-start(bf16[16,8192]{1,0:T(8,128)(2,1)} %add_convert_fusion.2), channel_id=1, source_target_pairs={{32,0},{64,32},{96,64},{128,96},{160,128},{192,160},{224,192},{256... | collective-permute-start | bytes 786440 | tf_op jit(solution)/shard_map/while/body/eval_jaxpr/ppermute | solution.py:22
  189.1 8.5 %collective-permute-start = (bf16[16,8192]{1,0:T(8,128)(2,1)}, bf16[16,8192]{1,0:T(8,128)(2,1)S(1)}, u32[]{:S(2)}, u32[]{:S(2)}) collective-permute-start(bf16[16,8192]{1,0:T(8,128)(2,1)} %add_convert_fusion.2), channel_id=1, source_target_pairs={{32,0},{64,32},{96,64},{128,96},{160,128},{192,160},{224,192},{256... | collective-permute-start | bytes 786440 | tf_op jit(solution)/shard_map/while/body/eval_jaxpr/ppermute | solution.py:22
  202.5 9.6 %collective-permute-start = (bf16[16,8192]{1,0:T(8,128)(2,1)}, bf16[16,8192]{1,0:T(8,128)(2,1)S(1)}, u32[]{:S(2)}, u32[]{:S(2)}) collective-permute-start(bf16[16,8192]{1,0:T(8,128)(2,1)} %add_convert_fusion.2), channel_id=1, source_target_pairs={{32,0},{64,32},{96,64},{128,96},{160,128},{192,160},{224,192},{256... | collective-permute-start | bytes 786440 | tf_op jit(solution)/shard_map/while/body/eval_jaxpr/ppermute | solution.py:22
  217.0 11.2 %collective-permute-start = (bf16[16,8192]{1,0:T(8,128)(2,1)}, bf16[16,8192]{1,0:T(8,128)(2,1)S(1)}, u32[]{:S(2)}, u32[]{:S(2)}) collective-permute-start(bf16[16,8192]{1,0:T(8,128)(2,1)} %add_convert_fusion.2), channel_id=1, source_target_pairs={{32,0},{64,32},{96,64},{128,96},{160,128},{192,160},{224,192},{256... | collective-permute-start | bytes 786440 | tf_op jit(solution)/shard_map/while/body/eval_jaxpr/ppermute | solution.py:22
  233.1 12.0 %collective-permute-start = (bf16[16,8192]{1,0:T(8,128)(2,1)}, bf16[16,8192]{1,0:T(8,128)(2,1)S(1)}, u32[]{:S(2)}, u32[]{:S(2)}) collective-permute-start(bf16[16,8192]{1,0:T(8,128)(2,1)} %add_convert_fusion.2), channel_id=1, source_target_pairs={{32,0},{64,32},{96,64},{128,96},{160,128},{192,160},{224,192},{256... | collective-permute-start | bytes 786440 | tf_op jit(solution)/shard_map/while/body/eval_jaxpr/ppermute | solution.py:22
  250.0 11.1 %collective-permute-start = (bf16[16,8192]{1,0:T(8,128)(2,1)}, bf16[16,8192]{1,0:T(8,128)(2,1)S(1)}, u32[]{:S(2)}, u32[]{:S(2)}) collective-permute-start(bf16[16,8192]{1,0:T(8,128)(2,1)} %add_convert_fusion.2), channel_id=1, source_target_pairs={{32,0},{64,32},{96,64},{128,96},{160,128},{192,160},{224,192},{256... | collective-permute-start | bytes 786440 | tf_op jit(solution)/shard_map/while/body/eval_jaxpr/ppermute | solution.py:22
  266.0 9.5 %collective-permute-start = (bf16[16,8192]{1,0:T(8,128)(2,1)}, bf16[16,8192]{1,0:T(8,128)(2,1)S(1)}, u32[]{:S(2)}, u32[]{:S(2)}) collective-permute-start(bf16[16,8192]{1,0:T(8,128)(2,1)} %add_convert_fusion.2), channel_id=1, source_target_pairs={{32,0},{64,32},{96,64},{128,96},{160,128},{192,160},{224,192},{256... | collective-permute-start | bytes 786440 | tf_op jit(solution)/shard_map/while/body/eval_jaxpr/ppermute | solution.py:22
  280.4 8.0 %collective-permute-start = (bf16[16,8192]{1,0:T(8,128)(2,1)}, bf16[16,8192]{1,0:T(8,128)(2,1)S(1)}, u32[]{:S(2)}, u32[]{:S(2)}) collective-permute-start(bf16[16,8192]{1,0:T(8,128)(2,1)} %add_convert_fusion.2), channel_id=1, source_target_pairs={{32,0},{64,32},{96,64},{128,96},{160,128},{192,160},{224,192},{256... | collective-permute-start | bytes 786440 | tf_op jit(solution)/shard_map/while/body/eval_jaxpr/ppermute | solution.py:22
  293.3 7.6 %collective-permute-start = (bf16[16,8192]{1,0:T(8,128)(2,1)}, bf16[16,8192]{1,0:T(8,128)(2,1)S(1)}, u32[]{:S(2)}, u32[]{:S(2)}) collective-permute-start(bf16[16,8192]{1,0:T(8,128)(2,1)} %add_convert_fusion.2), channel_id=1, source_target_pairs={{32,0},{64,32},{96,64},{128,96},{160,128},{192,160},{224,192},{256... | collective-permute-start | bytes 786440 | tf_op jit(solution)/shard_map/while/body/eval_jaxpr/ppermute | solution.py:22
  305.9 8.2 %collective-permute-start = (bf16[16,8192]{1,0:T(8,128)(2,1)}, bf16[16,8192]{1,0:T(8,128)(2,1)S(1)}, u32[]{:S(2)}, u32[]{:S(2)}) collective-permute-start(bf16[16,8192]{1,0:T(8,128)(2,1)} %add_convert_fusion.2), channel_id=1, source_target_pairs={{32,0},{64,32},{96,64},{128,96},{160,128},{192,160},{224,192},{256... | collective-permute-start | bytes 786440 | tf_op jit(solution)/shard_map/while/body/eval_jaxpr/ppermute | solution.py:22
  319.0 8.5 %collective-permute-start = (bf16[16,8192]{1,0:T(8,128)(2,1)}, bf16[16,8192]{1,0:T(8,128)(2,1)S(1)}, u32[]{:S(2)}, u32[]{:S(2)}) collective-permute-start(bf16[16,8192]{1,0:T(8,128)(2,1)} %add_convert_fusion.2), channel_id=1, source_target_pairs={{32,0},{64,32},{96,64},{128,96},{160,128},{192,160},{224,192},{256... | collective-permute-start | bytes 786440 | tf_op jit(solution)/shard_map/while/body/eval_jaxpr/ppermute | solution.py:22
  332.4 8.5 %collective-permute-start = (bf16[16,8192]{1,0:T(8,128)(2,1)}, bf16[16,8192]{1,0:T(8,128)(2,1)S(1)}, u32[]{:S(2)}, u32[]{:S(2)}) collective-permute-start(bf16[16,8192]{1,0:T(8,128)(2,1)} %add_convert_fusion.2), channel_id=1, source_target_pairs={{32,0},{64,32},{96,64},{128,96},{160,128},{192,160},{224,192},{256... | collective-permute-start | bytes 786440 | tf_op jit(solution)/shard_map/while/body/eval_jaxpr/ppermute | solution.py:22
  345.9 8.5 %collective-permute-start = (bf16[16,8192]{1,0:T(8,128)(2,1)}, bf16[16,8192]{1,0:T(8,128)(2,1)S(1)}, u32[]{:S(2)}, u32[]{:S(2)}) collective-permute-start(bf16[16,8192]{1,0:T(8,128)(2,1)} %add_convert_fusion.2), channel_id=1, source_target_pairs={{32,0},{64,32},{96,64},{128,96},{160,128},{192,160},{224,192},{256... | collective-permute-start | bytes 786440 | tf_op jit(solution)/shard_map/while/body/eval_jaxpr/ppermute | solution.py:22
  359.3 8.5 %collective-permute-start = (bf16[16,8192]{1,0:T(8,128)(2,1)}, bf16[16,8192]{1,0:T(8,128)(2,1)S(1)}, u32[]{:S(2)}, u32[]{:S(2)}) collective-permute-start(bf16[16,8192]{1,0:T(8,128)(2,1)} %add_convert_fusion.2), channel_id=1, source_target_pairs={{32,0},{64,32},{96,64},{128,96},{160,128},{192,160},{224,192},{256... | collective-permute-start | bytes 786440 | tf_op jit(solution)/shard_map/while/body/eval_jaxpr/ppermute | solution.py:22
  367.8 1.0 copy-start.5
  367.9 1.7 copy-start.2
  368.8 1.6 copy-start.4
  373.9 1.1 copy-start.7
  377.4 179.6 %all-gather.4.cloned.1.call-start = ((), (), s32[]{:S(2)}) async-start(), calls=%async_computation.3 | async-start | bytes 1474560 | tf_op jit(solution)/shard_map/all_gather | solution.py:106
Sparse Core Ops, SparseCore 0:
  377.5 70.5 reduce-scatter.1
  450.2 31.4 all-gather.3
